TPU v7x, 32 devices: a whole 2x2x4 slice. The times are simulated.
32 devices in a mesh: axial: 16 (over z, y, x), radial: 2 (over core).
Axes of the slice: x: 2, y: 2, z: 4, core: 2. Of those that a mesh axis runs over, the one named last changes fastest.
Arguments:
- parcel_load: float32 [5, 524288], P(None, ('axial', 'radial')), may hold values from -6 to 6
- parcel_offset: float32 [3, 524288], P(None, ('axial', 'radial')), may hold values from 0 to 1
- parcel_cell: int32 [524288], P(('axial', 'radial')), may hold values from 0 to 63
- cross_rows: int32 [2, 262144], P(None, ('axial', 'radial')), may hold values from -1 to 16383, as said below
- block_brick: int32 [8192], P(('axial', 'radial')), may hold values from 0 to 1023
- gas: float32 [5, 64, 128, 256], P(None, 'axial', 'radial'), may hold values from -6 to 6
Outputs:
- source: float32 [5, 64, 128, 256], P(None, 'axial', 'radial')
- parcel_gas: bfloat16 [5, 1048576], P(None, ('axial', 'radial'))
Inputs may be any that keep to these rules, and one draw needn't show every extreme that they name: `cross_rows`: on each half slab the non-empty entries of a list come first, and all rows named in both lists are distinct; the upward lists of some half slabs are full with 8192 rows in every draw.
All inputs are finite; a program needn't handle non-finite values.
Results may differ from a plain program's by a relative error of at most 0.001.
Values sent between devices are 32-bit elements; how exact they have to be, the bound alone decides.
No kernel may reach another device: no remote copies, remote signals or barrier semaphores. Data moves between devices by JAX's collectives and lax.ppermute only.
A program may use at most 64 MiB of HBM per device.

v0:
```python
import math

import jax
import jax.numpy as jnp
from jax import lax
from jax.sharding import PartitionSpec as P

COUPLE = 0.5


def passed_along(block, axis, distance):
    devices = range(lax.axis_size(axis))
    route = [(i - distance, i) for i in devices if i - distance in devices]
    return lax.ppermute(block, axis, route)


def kernel_weights(cell_index, offsets):
    extent = jnp.arange(128, dtype=jnp.int32)
    brick_x = extent // 25
    brick_y = extent // 5 % 5
    brick_z = extent % 5
    inside = (extent < 125).astype(jnp.float32)

    def factor(cell_coord, brick_coord, fraction):
        cell_coord = cell_coord[:, :, None]
        fraction = fraction[:, :, None]
        return jnp.where(
            brick_coord == cell_coord,
            1.0 - fraction,
            jnp.where(brick_coord == cell_coord + 1, fraction, 0.0),
        )

    cell_x = cell_index // 16
    cell_y = cell_index // 4 % 4
    cell_z = cell_index % 4
    return (
        factor(cell_x, brick_x, offsets[0])
        * factor(cell_y, brick_y, offsets[1])
        * factor(cell_z, brick_z, offsets[2])
        * inside
    )


def split_windows(field, axis, count):
    core = lax.slice_in_dim(field, 0, 4 * count, axis=axis)
    core = core.reshape(field.shape[:axis] + (count, 4) + field.shape[axis + 1 :])
    tail = lax.slice_in_dim(field, 4, 4 * count + 1, stride=4, axis=axis)
    tail = jnp.expand_dims(tail, axis + 1)
    return jnp.concatenate([core, tail], axis + 1)


def merge_windows(field, axis, count, keep_tail):
    core = lax.slice_in_dim(field, 0, 4, axis=axis + 1)
    tail = lax.slice_in_dim(field, 4, 5, axis=axis + 1)
    zero_brick = jnp.zeros_like(lax.slice_in_dim(core, 0, 1, axis=axis))
    core = jnp.concatenate([core, zero_brick], axis)
    zero_tail = jnp.zeros_like(lax.slice_in_dim(tail, 0, 1, axis=axis))
    tail = jnp.concatenate([zero_tail, tail], axis)
    first = lax.slice_in_dim(core, 0, 1, axis=axis + 1) + tail
    rest = lax.slice_in_dim(core, 1, 4, axis=axis + 1)
    joined = jnp.concatenate([first, rest], axis + 1)
    joined = joined.reshape(field.shape[:axis] + (4 * (count + 1),) + field.shape[axis + 2 :])
    length = 4 * count + 1 if keep_tail else 4 * count
    return lax.slice_in_dim(joined, 0, length, axis=axis)


def radial_fold(layers):
    arrived = passed_along(layers[:, :, -1], "radial", 1)
    return layers.at[:, :, 0].add(arrived)


def departed_mask(cross_rows, resident):
    rows = cross_rows.reshape(-1)
    lanes = 128
    high = jnp.where(rows >= 0, rows // lanes, -1)
    low = jnp.where(rows >= 0, rows % lanes, -1)
    high_hot = (high[:, None] == jnp.arange(resident // lanes, dtype=jnp.int32)[None, :]).astype(jnp.bfloat16)
    low_hot = (low[:, None] == jnp.arange(lanes, dtype=jnp.int32)[None, :]).astype(jnp.bfloat16)
    counts = jnp.einsum("sh,sl->hl", high_hot, low_hot, preferred_element_type=jnp.float32)
    return counts.reshape(resident)


def per_device(parcel_load, parcel_offset, parcel_cell, cross_rows, block_brick, gas):
    span_x = gas.shape[1]
    span_y = gas.shape[2]
    span_z = gas.shape[3]
    count_x = span_x // 4
    count_y = span_y // 4
    count_z = span_z // 4
    brick_total = count_x * count_y * count_z
    resident = parcel_load.shape[1]
    block_count = block_brick.shape[0]
    group_size = math.gcd(block_count, 64)
    turn_count = block_count // group_size
    brick_numbers = jnp.arange(brick_total, dtype=jnp.int32)
    attributes = jnp.concatenate(
        [parcel_load, parcel_offset, parcel_cell[None].astype(jnp.float32)], 0
    )
    usable = cross_rows >= 0
    safe_rows = jnp.maximum(cross_rows, 0)
    upward = attributes[:, safe_rows[0]] * usable[0].astype(jnp.float32)
    downward = attributes[:, safe_rows[1]] * usable[1].astype(jnp.float32)
    from_lower = passed_along(upward, "axial", 1)
    from_upper = passed_along(downward, "axial", -1)
    departed = departed_mask(cross_rows, resident)
    staying = jnp.concatenate([attributes[:8] * (1.0 - departed)[None], attributes[8:]], 0)
    parcels = jnp.concatenate([staying, from_lower, from_upper], 1)

    def group_pieces(turn_index):
        first_block = turn_index * group_size
        parcel_part = lax.dynamic_slice_in_dim(parcels, first_block * 128, group_size * 128, 1)
        brick_ids = lax.dynamic_slice_in_dim(block_brick, first_block, group_size, 0)
        block_rows = parcel_part.reshape(9, group_size, 128)
        weights = kernel_weights(block_rows[8].astype(jnp.int32), block_rows[5:8])
        selector = (brick_ids[:, None] == brick_numbers[None, :]).astype(jnp.float32)
        return (block_rows, weights, selector)

    def deposit_turn(turn_index, brick_sums):
        block_rows, weights, selector = group_pieces(turn_index)
        spread = jnp.einsum(
            "fgp,gpe->fge", block_rows[:5], weights, precision=lax.Precision.HIGHEST
        )
        return brick_sums + jnp.einsum(
            "gb,fge->fbe", selector, spread, precision=lax.Precision.HIGHEST
        )

    brick_sums = lax.fori_loop(
        0, turn_count, deposit_turn, jnp.zeros((5, brick_total, 128), jnp.float32)
    )
    laid = brick_sums[:, :, :125].reshape(5, count_x, count_y, count_z, 5, 5, 5)
    laid = jnp.transpose(laid, (0, 1, 4, 2, 5, 3, 6))
    laid = merge_windows(laid, 1, count_x, True)
    laid = merge_windows(laid, 2, count_y, True)
    deposit_grid = merge_windows(laid, 3, count_z, False)
    incoming = passed_along(deposit_grid[:, span_x], "axial", 1)
    summed = deposit_grid[:, :span_x].at[:, 0].add(incoming)
    folded = radial_fold(summed)
    source = folded[:, :, :span_y]
    updated_gas = gas + COUPLE * source
    upper_face = passed_along(updated_gas[:, 0], "axial", -1)
    extended = jnp.concatenate([updated_gas, upper_face[:, None]], 1)
    below_row = passed_along(extended[:, :, 0], "radial", -1)
    gas_field = jnp.concatenate([extended, below_row[:, :, None]], 2)
    gas_field = jnp.pad(gas_field, ((0, 0), (0, 0), (0, 0), (0, 1)))
    windows = split_windows(gas_field, 3, count_z)
    windows = split_windows(windows, 2, count_y)
    windows = split_windows(windows, 1, count_x)
    windows = jnp.transpose(windows, (0, 1, 3, 5, 2, 4, 6)).reshape(5, brick_total, 125)
    brick_gas = jnp.pad(windows, ((0, 0), (0, 0), (0, 3)))

    def sample_turn(turn_index, sampled):
        block_rows, weights, selector = group_pieces(turn_index)
        picked = jnp.einsum("gb,fbe->fge", selector, brick_gas, precision=lax.Precision.HIGHEST)
        values = jnp.einsum("fge,gpe->fgp", picked, weights, precision=lax.Precision.HIGHEST)
        values = values.reshape(5, group_size * 128).astype(jnp.bfloat16)
        return lax.dynamic_update_slice_in_dim(sampled, values, turn_index * group_size * 128, 1)

    parcel_gas = lax.fori_loop(
        0, turn_count, sample_turn, jnp.zeros((5, parcels.shape[1]), jnp.bfloat16)
    )
    return (source, parcel_gas)


def solution(mesh):
    return jax.shard_map(
        per_device,
        mesh=mesh,
        in_specs=(
            P(None, ("axial", "radial")),
            P(None, ("axial", "radial")),
            P(("axial", "radial")),
            P(None, ("axial", "radial")),
            P(("axial", "radial")),
            P(None, "axial", "radial", None),
        ),
        out_specs=(P(None, "axial", "radial", None), P(None, ("axial", "radial"))),
        check_vma=False,
    )
```

profile of v0, /device:TPU:23, one launch (start us, length us, event | category | flops | bytes accessed | tf_op | source)
XLA Modules:
  0.0 491.4 jit_solution(9939889142905646769)
XLA Ops:
  9.4 31.3 %gather_fusion = f32[8192,9]{1,0:T(8,128)} fusion(f32[9,16384]{0,1:T(8,128)} %copy.70, s32[8192]{0:T(1024)S(1)} %broadcast_clamp_fusion.1), kind=kCustom, calls=%fused_computation | custom fusion | bytes 622592 | tf_op jit(solution)/shard_map/gather | solution.py:101
  51.5 31.3 %gather_fusion.1 = f32[8192,9]{1,0:T(8,128)} fusion(f32[9,16384]{0,1:T(8,128)} %copy.70, s32[8192]{0:T(1024)S(1)} %broadcast_clamp_fusion), kind=kCustom, calls=%fused_computation.1 | custom fusion | bytes 622592 | tf_op jit(solution)/shard_map/gather | solution.py:102
  101.1 6.1 %collective-permute-done.1 = f32[9,8192]{1,0:T(8,128)} collective-permute-done((f32[9,8192]{1,0:T(8,128)}, f32[9,8192]{1,0:T(8,128)}, u32[]{:S(2)}, u32[]{:S(2)}) %collective-permute-start.1) | collective-permute-done | bytes 294944 | tf_op jit(solution)/shard_map/ppermute | solution.py:14
  109.9 86.5 %while.37 = (s32[]{:T(128)}, f32[5,1024,128]{1,2,0:T(8,128)S(1)}, f32[9,32768]{1,0:T(8,128)}, s32[256]{0:T(256)S(1)}, s32[]{:T(128)}, /*index=5*/s32[]{:T(128)},...) while((s32[]{:T(128)}, f32[5,1024,128]{1,2,0:T(8,128)S(1)}, ...), condition=%wide.region_1.2_spmd.clone, body=%wide.region_0.1_spmd.clone.sunk | while | flops 583724544 | bytes 6919223 | solution.py:127
  111.5 18.0 %fusion.151 = f32[5,64,128]{2,0,1:T(8,128)S(1)} fusion(f32[128]{0:T(128)S(1)} %compare_convert_fusion.5, f32[64,128]{1,0:T(8,128)S(1)} %bitcast.156, s32[64,128]{1,0:T(8,128)S(1)} %get-tuple-element.606, f32[64,128]{1,0:T(8,128)S(1)} %get-tuple-element.608, s32[64,128]{1,0:T(8,128)S(1)} %get-tuple-element.609, s32[128]{0:T(128)S(1)} %get-tuple-element.610, ...), kind=kOutput, calls=%fused_computation.114.clone.3 | convolution fusion | flops 78643200 | bytes 821252 | tf_op jit(solution)/shard_map/while/body/eval_jaxpr/fgp,gpe->fge/dot_general | solution.py:120
  133.1 18.0 %fusion.151 = f32[5,64,128]{2,0,1:T(8,128)S(1)} fusion(f32[128]{0:T(128)S(1)} %compare_convert_fusion.5, f32[64,128]{1,0:T(8,128)S(1)} %bitcast.156, s32[64,128]{1,0:T(8,128)S(1)} %get-tuple-element.606, f32[64,128]{1,0:T(8,128)S(1)} %get-tuple-element.608, s32[64,128]{1,0:T(8,128)S(1)} %get-tuple-element.609, s32[128]{0:T(128)S(1)} %get-tuple-element.610, ...), kind=kOutput, calls=%fused_computation.114.clone.3 | convolution fusion | flops 78643200 | bytes 821252 | tf_op jit(solution)/shard_map/while/body/eval_jaxpr/fgp,gpe->fge/dot_general | solution.py:120
  154.7 18.0 %fusion.151 = f32[5,64,128]{2,0,1:T(8,128)S(1)} fusion(f32[128]{0:T(128)S(1)} %compare_convert_fusion.5, f32[64,128]{1,0:T(8,128)S(1)} %bitcast.156, s32[64,128]{1,0:T(8,128)S(1)} %get-tuple-element.606, f32[64,128]{1,0:T(8,128)S(1)} %get-tuple-element.608, s32[64,128]{1,0:T(8,128)S(1)} %get-tuple-element.609, s32[128]{0:T(128)S(1)} %get-tuple-element.610, ...), kind=kOutput, calls=%fused_computation.114.clone.3 | convolution fusion | flops 78643200 | bytes 821252 | tf_op jit(solution)/shard_map/while/body/eval_jaxpr/fgp,gpe->fge/dot_general | solution.py:120
  176.3 18.0 %fusion.151 = f32[5,64,128]{2,0,1:T(8,128)S(1)} fusion(f32[128]{0:T(128)S(1)} %compare_convert_fusion.5, f32[64,128]{1,0:T(8,128)S(1)} %bitcast.156, s32[64,128]{1,0:T(8,128)S(1)} %get-tuple-element.606, f32[64,128]{1,0:T(8,128)S(1)} %get-tuple-element.608, s32[64,128]{1,0:T(8,128)S(1)} %get-tuple-element.609, s32[128]{0:T(128)S(1)} %get-tuple-element.610, ...), kind=kOutput, calls=%fused_computation.114.clone.3 | convolution fusion | flops 78643200 | bytes 821252 | tf_op jit(solution)/shard_map/while/body/eval_jaxpr/fgp,gpe->fge/dot_general | solution.py:120
  210.7 5.9 %reshape.644 = f32[5,5,68,64,5]{3,2,4,1,0:T(8,128)} reshape(f32[5,5,17,4,64,5]{4,3,2,5,1,0:T(4,128)} %copy.74) | data formatting | bytes 4352000 | tf_op jit(solution)/shard_map/reshape | solution.py:62
  222.8 6.0 %copy.75 = f32[5,5,65,65,4]{2,4,3,1,0:T(4,128)} copy(f32[5,5,65,65,4]{3,2,4,1,0:T(8,128)} %pad_maximum_fusion.3) | data formatting | bytes 3380000 | tf_op jit(solution)/shard_map/concatenate | solution.py:61
  238.8 6.8 %collective-permute-done.2 = f32[5,65,256]{2,1,0:T(8,128)} collective-permute-done((f32[5,65,256]{2,1,0:T(8,128)}, f32[5,65,256]{2,1,0:T(8,128)}, u32[]{:S(2)}, u32[]{:S(2)}) %collective-permute-start.2) | collective-permute-done | bytes 332832 | tf_op jit(solution)/shard_map/ppermute | solution.py:14
  262.6 6.9 %scatter-add.9 = f32[5,4,65,256]{2,3,1,0:T(8,128)} dynamic-update-slice(f32[5,4,65,256]{2,3,1,0:T(8,128)} %fusion.115, f32[5,4,1,256]{2,3,1,0:T(8,128)S(1)} %slice_add_fusion, s32[]{:T(128)} %constant.556.clone.1, s32[]{:T(128)} %constant.556.clone.1, s32[]{:T(128)} %constant.556.clone.1, s32[]{:T(128)} %constant.556.clone.1) | dynamic-update-slice | bytes 40964 | tf_op jit(solution)/shard_map/scatter-add | solution.py:69
  277.2 8.8 %collective-permute-done.4 = f32[5,64,256]{2,1,0:T(8,128)} collective-permute-done((f32[5,64,256]{2,1,0:T(8,128)}, f32[5,64,256]{2,1,0:T(8,128)}, u32[]{:S(2)}, u32[]{:S(2)}) %collective-permute-start.4) | collective-permute-done | bytes 327712 | tf_op jit(solution)/shard_map/ppermute | solution.py:14
  288.1 5.1 %collective-permute-start.5 = (f32[5,5,256]{2,1,0:T(8,128)S(1)}, f32[5,5,256]{2,1,0:T(8,128)S(1)}, u32[]{:S(2)}, u32[]{:S(2)}) collective-permute-start(f32[5,5,256]{2,1,0:T(8,128)S(1)} %fusion.108), channel_id=1, source_target_pairs={{1,0},{3,2},{5,4},{7,6},{9,8},{11,10},{13,12},{15,14},{17,16},{19,... | collective-permute-start | bytes 76808 | tf_op jit(solution)/shard_map/ppermute | solution.py:14
  303.0 6.6 %slice.301 = f32[5,5,65,64]{2,3,1,0:T(8,128)} slice(f32[5,5,65,257]{2,3,1,0:T(8,128)} %select_maximum_fusion), slice={[0:5:1], [0:5:1], [0:65:1], [4:257:4]} | slice | bytes 832000 | tf_op jit(solution)/shard_map/slice | solution.py:47
  309.6 5.7 %concatenate.93 = f32[5,5,1,64,4]{2,4,3,1,0:T(4,128)} reshape(f32[5,5,256]{2,1,0:T(8,128)S(1)} %collective-permute-done.5) | data formatting | bytes 51200 | tf_op jit(solution)/shard_map/concatenate | solution.py:143
  315.3 5.8 %pad_maximum_fusion.1 = f32[5,5,65,64,5]{2,4,3,1,0:T(8,128)} fusion(f32[5,5,65,64,1]{2,4,3,1,0:T(1,128)} %bitcast.146, f32[5,5,1,64,4]{2,4,3,1,0:T(4,128)} %concatenate.93, f32[5,1,64,64,4]{2,4,3,1,0:T(4,128)S(1)} %bitcast.143, f32[5,4,64,64,4]{2,4,3,1,0:T(4,128)S(1)} %bitcast.133), kind=kLoop, calls=%fused_computation.169 | loop fusion | flops 1560000 | bytes 4160000 | tf_op jit(solution)/shard_map/concatenate | solution.py:49
  321.0 49.2 %slice.303 = f32[5,5,16,64,5]{2,4,3,1,0:T(8,128)} slice(f32[5,5,65,64,5]{2,4,3,1,0:T(8,128)} %pad_maximum_fusion.1), slice={[0:5:1], [0:5:1], [4:65:4], [0:64:1], [0:5:1]} | slice | bytes 1024000 | tf_op jit(solution)/shard_map/slice | solution.py:47
  375.1 7.0 %copy.87 = f32[5,5,64,64,5]{3,2,4,1,0:T(8,128)} copy(f32[5,5,64,64,5]{2,4,3,1,0:T(8,128)} %bitcast.132) | data formatting | bytes 4096000 | tf_op jit(solution)/shard_map/slice | solution.py:45
  398.7 91.7 %while.36 = (s32[]{:T(128)}, bf16[5,32768]{1,0:T(8,128)(2,1)S(1)}, f32[9,32768]{1,0:T(8,128)}, s32[256]{0:T(256)S(1)}, f32[5,1024,128]{2,1,0:T(8,128)S(1)}, /*in...) while((s32[]{:T(128)}, bf16[5,32768]{1,0:T(8,128)(2,1)S(1)}, ...), condition=%wide.region_3.4_spmd.clone, body=%wide.region_2.3_spmd.clone.sunk | while | flops 582454784 | bytes 4166709 | solution.py:158
  401.9 19.9 %fusion.146 = bf16[5,32768]{1,0:T(8,128)(2,1)S(1)} fusion(bf16[5,32768]{1,0:T(8,128)(2,1)S(1)} %get-tuple-element.676, s32[]{:T(128)S(6)} %select_n.843, f32[128]{0:T(128)S(1)} %compare_convert_fusion.4, f32[64,128]{1,0:T(8,128)S(1)} %bitcast.154, s32[64,128]{1,0:T(8,128)S(1)} %get-tuple-element.588, f32[64,128]{1,0:T(8,128)S(1)} %get-tuple-element.590, ...), kind=kOutput, calls=%fused_computation.39.clone.2 | convolution fusion | flops 78684160 | bytes 690180 | tf_op jit(solution)/shard_map/while/body/eval_jaxpr/fge,gpe->fgp/dot_general | solution.py:154
  424.7 19.9 %fusion.146 = bf16[5,32768]{1,0:T(8,128)(2,1)S(1)} fusion(bf16[5,32768]{1,0:T(8,128)(2,1)S(1)} %get-tuple-element.676, s32[]{:T(128)S(6)} %select_n.843, f32[128]{0:T(128)S(1)} %compare_convert_fusion.4, f32[64,128]{1,0:T(8,128)S(1)} %bitcast.154, s32[64,128]{1,0:T(8,128)S(1)} %get-tuple-element.588, f32[64,128]{1,0:T(8,128)S(1)} %get-tuple-element.590, ...), kind=kOutput, calls=%fused_computation.39.clone.2 | convolution fusion | flops 78684160 | bytes 690180 | tf_op jit(solution)/shard_map/while/body/eval_jaxpr/fge,gpe->fgp/dot_general | solution.py:154
  447.6 19.9 %fusion.146 = bf16[5,32768]{1,0:T(8,128)(2,1)S(1)} fusion(bf16[5,32768]{1,0:T(8,128)(2,1)S(1)} %get-tuple-element.676, s32[]{:T(128)S(6)} %select_n.843, f32[128]{0:T(128)S(1)} %compare_convert_fusion.4, f32[64,128]{1,0:T(8,128)S(1)} %bitcast.154, s32[64,128]{1,0:T(8,128)S(1)} %get-tuple-element.588, f32[64,128]{1,0:T(8,128)S(1)} %get-tuple-element.590, ...), kind=kOutput, calls=%fused_computation.39.clone.2 | convolution fusion | flops 78684160 | bytes 690180 | tf_op jit(solution)/shard_map/while/body/eval_jaxpr/fge,gpe->fgp/dot_general | solution.py:154
  470.4 19.9 %fusion.146 = bf16[5,32768]{1,0:T(8,128)(2,1)S(1)} fusion(bf16[5,32768]{1,0:T(8,128)(2,1)S(1)} %get-tuple-element.676, s32[]{:T(128)S(6)} %select_n.843, f32[128]{0:T(128)S(1)} %compare_convert_fusion.4, f32[64,128]{1,0:T(8,128)S(1)} %bitcast.154, s32[64,128]{1,0:T(8,128)S(1)} %get-tuple-element.588, f32[64,128]{1,0:T(8,128)S(1)} %get-tuple-element.590, ...), kind=kOutput, calls=%fused_computation.39.clone.2 | convolution fusion | flops 78684160 | bytes 690180 | tf_op jit(solution)/shard_map/while/body/eval_jaxpr/fge,gpe->fgp/dot_general | solution.py:154
  (156 shorter events, 155.4 us)
Async XLA Ops:
  48.4 52.7 %collective-permute-start = (f32[9,8192]{1,0:T(8,128)}, f32[9,8192]{1,0:T(8,128)}, u32[]{:S(2)}, u32[]{:S(2)}) collective-permute-start(f32[9,8192]{1,0:T(8,128)} %copy.71), channel_id=1, source_target_pairs={{0,2},{2,4},{4,6},{6,8},{8,10},{10,12},{12,14},{14,16},{16,18},{18... | collective-permute-start | bytes 884744 | tf_op jit(solution)/shard_map/ppermute | solution.py:14
  87.0 6.4 %copy-start.3 = (s32[2,8192]{1,0:T(2,128)S(1)}, s32[2,8192]{1,0:T(2,128)}, u32[]{:S(2)}) copy-start(s32[2,8192]{1,0:T(2,128)} %param.17) | copy-start | bytes 196612
  90.5 10.4 %copy-start.1 = (f32[5,16384]{1,0:T(8,128)S(1)}, f32[5,16384]{1,0:T(8,128)}, u32[]{:S(2)}) copy-start(f32[5,16384]{1,0:T(8,128)} %param.14) | copy-start | bytes 983044
  90.5 10.4 %copy-start.2 = (f32[3,16384]{1,0:T(4,128)S(1)}, f32[3,16384]{1,0:T(4,128)}, u32[]{:S(2)}) copy-start(f32[3,16384]{1,0:T(4,128)} %param.15) | copy-start | bytes 589828
  90.5 16.7 %collective-permute-start.1 = (f32[9,8192]{1,0:T(8,128)}, f32[9,8192]{1,0:T(8,128)}, u32[]{:S(2)}, u32[]{:S(2)}) collective-permute-start(f32[9,8192]{1,0:T(8,128)} %copy.73), channel_id=1, source_target_pairs={{2,0},{4,2},{6,4},{8,6},{10,8},{12,10},{14,12},{16,14},{18,16},{20... | collective-permute-start | bytes 884744 | tf_op jit(solution)/shard_map/ppermute | solution.py:14
  96.3 13.6 %copy-start.5 = (s32[256]{0:T(256)S(1)}, s32[256]{0:T(256)}, u32[]{:S(2)}) copy-start(s32[256]{0:T(256)} %param.18) | copy-start | bytes 3076
  235.1 10.5 %collective-permute-start.2 = (f32[5,65,256]{2,1,0:T(8,128)}, f32[5,65,256]{2,1,0:T(8,128)}, u32[]{:S(2)}, u32[]{:S(2)}) collective-permute-start(f32[5,65,256]{2,1,0:T(8,128)} %copy.76), channel_id=1, source_target_pairs={{0,2},{2,4},{4,6},{6,8},{8,10},{10,12},{12,14},{14,16},{16,18},{18... | collective-permute-start | bytes 998408 | tf_op jit(solution)/shard_map/ppermute | solution.py:14
  253.0 4.6 collective-permute-start.3
  275.1 10.9 %collective-permute-start.4 = (f32[5,64,256]{2,1,0:T(8,128)}, f32[5,64,256]{2,1,0:T(8,128)}, u32[]{:S(2)}, u32[]{:S(2)}) collective-permute-start(f32[5,64,256]{2,1,0:T(8,128)} %copy.80), channel_id=1, source_target_pairs={{2,0},{4,2},{6,4},{8,6},{10,8},{12,10},{14,12},{16,14},{18,16},{20... | collective-permute-start | bytes 983048 | tf_op jit(solution)/shard_map/ppermute | solution.py:14
  288.1 8.1 %collective-permute-start.5 = (f32[5,5,256]{2,1,0:T(8,128)S(1)}, f32[5,5,256]{2,1,0:T(8,128)S(1)}, u32[]{:S(2)}, u32[]{:S(2)}) collective-permute-start(f32[5,5,256]{2,1,0:T(8,128)S(1)} %fusion.108), channel_id=1, source_target_pairs={{1,0},{3,2},{5,4},{7,6},{9,8},{11,10},{13,12},{15,14},{17,16},{19,... | collective-permute-start | bytes 76808 | tf_op jit(solution)/shard_map/ppermute | solution.py:14
  382.1 3.2 copy-start
  490.4 0.8 copy-start.4
where the time goes:
time: 499 us; the launch traced here: 491 us
  local copies, waits for them, and re-layouts  221 us (44%)
  matrix products  168 us (34%)
  other arithmetic  62.1 us (12%)
  waiting for transfers between devices  22 us (4%)
  starting transfers between devices  16.4 us (3%)
    dot_general x4, matrix products, sample_turn(): jnp.einsum('fge,gpe->fgp', picked, weights, precision=lax.Precision.HIGHEST)  79.7 us
    dot_general x4, matrix products, deposit_turn(): jnp.einsum('fgp,gpe->fge', block_rows[:5], weights, precision=lax.Precisi...  71.8 us
    slice x2, local copies, waits for them, and re-layouts, split_windows(): tail = lax.slice_in_dim(field, 4, 4 * count + 1, stride=4, axis=axis)  55.8 us
    gather x1, local copies, waits for them, and re-layouts, per_device(): upward = attributes[:, safe_rows[0]] * usable[0].astype(jnp.float32)  31.3 us
    gather x1, local copies, waits for them, and re-layouts, per_device(): downward = attributes[:, safe_rows[1]] * usable[1].astype(jnp.float32)  31.3 us
    ppermute x6, waiting for transfers between devices, passed_along(): return lax.ppermute(block, axis, route)  22 us
    ppermute x6, starting transfers between devices, passed_along(): return lax.ppermute(block, axis, route)  16.4 us
    slice x8, other arithmetic, kernel_weights(): offsets[0]  12.3 us
  transfers between devices with their start and end apart: 6, of which 4 were waited for; matrix products, arithmetic and copies ran while one was open for 11% of the time, Pallas kernels for 0%

commit v1 on v0

--- a/solution.py
+++ b/solution.py
@@ -62,6 +62,13 @@
     joined = joined.reshape(field.shape[:axis] + (4 * (count + 1),) + field.shape[axis + 2 :])
     length = 4 * count + 1 if keep_tail else 4 * count
     return lax.slice_in_dim(joined, 0, length, axis=axis)
+
+
+def window_map(count, length):
+    extent = jnp.arange(5, dtype=jnp.int32)[:, None, None]
+    brick = jnp.arange(count, dtype=jnp.int32)[None, :, None]
+    cell = jnp.arange(length, dtype=jnp.int32)[None, None, :]
+    return (4 * brick + extent == cell).astype(jnp.float32)
 
 
 def radial_fold(layers):
@@ -121,17 +128,29 @@
             "fgp,gpe->fge", block_rows[:5], weights, precision=lax.Precision.HIGHEST
         )
         return brick_sums + jnp.einsum(
-            "gb,fge->fbe", selector, spread, precision=lax.Precision.HIGHEST
+            "gb,fge->feb", selector, spread, precision=lax.Precision.HIGHEST
         )
 
     brick_sums = lax.fori_loop(
-        0, turn_count, deposit_turn, jnp.zeros((5, brick_total, 128), jnp.float32)
-    )
-    laid = brick_sums[:, :, :125].reshape(5, count_x, count_y, count_z, 5, 5, 5)
-    laid = jnp.transpose(laid, (0, 1, 4, 2, 5, 3, 6))
-    laid = merge_windows(laid, 1, count_x, True)
-    laid = merge_windows(laid, 2, count_y, True)
-    deposit_grid = merge_windows(laid, 3, count_z, False)
+        0, turn_count, deposit_turn, jnp.zeros((5, 128, brick_total), jnp.float32)
+    )
+    if count_x == 1:
+        laid = brick_sums[:, :125].reshape(5, 25, 5, count_y, count_z)
+        laid = jnp.einsum(
+            "faeyk,ekz->fayz", laid, window_map(count_z, span_z), precision=lax.Precision.HIGHEST
+        )
+        laid = laid.reshape(5, 5, 5, count_y, span_z)
+        deposit_grid = jnp.einsum(
+            "fxwyz,wyn->fxnz", laid, window_map(count_y, span_y + 1),
+            precision=lax.Precision.HIGHEST,
+        )
+    else:
+        laid = jnp.transpose(brick_sums[:, :125], (0, 2, 1))
+        laid = laid.reshape(5, count_x, count_y, count_z, 5, 5, 5)
+        laid = jnp.transpose(laid, (0, 1, 4, 2, 5, 3, 6))
+        laid = merge_windows(laid, 1, count_x, True)
+        laid = merge_windows(laid, 2, count_y, True)
+        deposit_grid = merge_windows(laid, 3, count_z, False)
     incoming = passed_along(deposit_grid[:, span_x], "axial", 1)
     summed = deposit_grid[:, :span_x].at[:, 0].add(incoming)
     folded = radial_fold(summed)
@@ -141,16 +160,29 @@
     extended = jnp.concatenate([updated_gas, upper_face[:, None]], 1)
     below_row = passed_along(extended[:, :, 0], "radial", -1)
     gas_field = jnp.concatenate([extended, below_row[:, :, None]], 2)
-    gas_field = jnp.pad(gas_field, ((0, 0), (0, 0), (0, 0), (0, 1)))
-    windows = split_windows(gas_field, 3, count_z)
-    windows = split_windows(windows, 2, count_y)
-    windows = split_windows(windows, 1, count_x)
-    windows = jnp.transpose(windows, (0, 1, 3, 5, 2, 4, 6)).reshape(5, brick_total, 125)
-    brick_gas = jnp.pad(windows, ((0, 0), (0, 0), (0, 3)))
+    if count_x == 1:
+        windows = jnp.einsum(
+            "fxnz,wyn->fxwyz", gas_field, window_map(count_y, span_y + 1),
+            precision=lax.Precision.HIGHEST,
+        )
+        windows = windows.reshape(5, 25, count_y, span_z)
+        windows = jnp.einsum(
+            "fayz,ekz->faeyk", windows, window_map(count_z, span_z),
+            precision=lax.Precision.HIGHEST,
+        )
+        windows = windows.reshape(5, 125, brick_total)
+    else:
+        gas_field = jnp.pad(gas_field, ((0, 0), (0, 0), (0, 0), (0, 1)))
+        windows = split_windows(gas_field, 3, count_z)
+        windows = split_windows(windows, 2, count_y)
+        windows = split_windows(windows, 1, count_x)
+        windows = jnp.transpose(windows, (0, 1, 3, 5, 2, 4, 6)).reshape(5, brick_total, 125)
+        windows = jnp.transpose(windows, (0, 2, 1))
+    brick_gas = jnp.pad(windows, ((0, 0), (0, 3), (0, 0)))
 
     def sample_turn(turn_index, sampled):
         block_rows, weights, selector = group_pieces(turn_index)
-        picked = jnp.einsum("gb,fbe->fge", selector, brick_gas, precision=lax.Precision.HIGHEST)
+        picked = jnp.einsum("gb,feb->fge", selector, brick_gas, precision=lax.Precision.HIGHEST)
         values = jnp.einsum("fge,gpe->fgp", picked, weights, precision=lax.Precision.HIGHEST)
         values = values.reshape(5, group_size * 128).astype(jnp.bfloat16)
         return lax.dynamic_update_slice_in_dim(sampled, values, turn_index * group_size * 128, 1)

time: 499 us -> 356 us (0.71); the launches traced: 491 us -> 355 us
  local copies, waits for them, and re-layouts: 221 us -> 93.8 us
  other arithmetic: 62.1 us -> 35.7 us
  matrix products: 168 us -> 181 us
  waiting for transfers between devices: 22 us -> 28.3 us
    slice x12 -> x0, local copies, waits for them, and re-layouts: 71.8 us -> none  [the longest x2 55.8 us: split_windows(): tail = lax.slice_in_dim(field, 4, 4 * count + 1, stride=4, axis=axis)]
    concatenate x3 -> x0, local copies, waits for them, and re-layouts: 14.9 us -> none  [the longest x2 9.19 us: merge_windows(): joined = jnp.concatenate([first, rest], axis + 1)]
    concatenate x5 -> x1, other arithmetic: 14.2 us -> 0.01 us  [per_device(): extended = jnp.concatenate([updated_gas, upper_face[:, None]], 1)]
    dot_general x8 -> x12, matrix products: 12 us -> 25.4 us  [the longest x4 7.27 us: deposit_turn(): jnp.einsum('gb,fge->feb', selector, spread, precision=lax.Precision.HIGHEST)]
    unnamed x16 -> x13, local copies, waits for them, and re-layouts: 8.95 us -> 0.85 us
    reshape x4 -> x2, local copies, waits for them, and re-layouts: 16.5 us -> 8.69 us  [the longest x1 5.05 us: per_device(): windows = windows.reshape(5, 125, brick_total)]
    ppermute x6, waiting for transfers between devices: 22 us -> 28.3 us  [passed_along(): return lax.ppermute(block, axis, route)]
    scatter-add x1, local copies, waits for them, and re-layouts: 6.87 us -> 1.72 us  [radial_fold(): return layers.at[:, :, 0].add(arrived)]
  transfers between devices with their start and end apart: 6 -> 6, of which waited for: 4 -> 5; matrix products, arithmetic and copies ran while one was open for 11% -> 13% of each run, Pallas kernels for 0% -> 0%
where the time goes in v1:
time: 356 us; the launch traced here: 355 us
  matrix products  181 us (51%)
  local copies, waits for them, and re-layouts  93.8 us (26%)
  other arithmetic  35.7 us (10%)
  waiting for transfers between devices  28.3 us (8%)
  starting transfers between devices  13.9 us (4%)
    dot_general x4, matrix products, sample_turn(): jnp.einsum('fge,gpe->fgp', picked, weights, precision=lax.Precision.HIGHEST)  79.7 us
    dot_general x4, matrix products, deposit_turn(): jnp.einsum('fgp,gpe->fge', block_rows[:5], weights, precision=lax.Precisi...  71.8 us
    gather x1, local copies, waits for them, and re-layouts, per_device(): upward = attributes[:, safe_rows[0]] * usable[0].astype(jnp.float32)  31.2 us
    gather x1, local copies, waits for them, and re-layouts, per_device(): downward = attributes[:, safe_rows[1]] * usable[1].astype(jnp.float32)  31.2 us
    ppermute x6, waiting for transfers between devices, passed_along(): return lax.ppermute(block, axis, route)  28.3 us
    ppermute x6, starting transfers between devices, passed_along(): return lax.ppermute(block, axis, route)  13.9 us
    slice x8, other arithmetic, kernel_weights(): offsets[0]  12.4 us
    dot_general x4, matrix products, deposit_turn(): jnp.einsum('gb,fge->feb', selector, spread, precision=lax.Precision.HIGHEST)  7.27 us
  transfers between devices with their start and end apart: 6, of which 5 were waited for; matrix products, arithmetic and copies ran while one was open for 13% of the time, Pallas kernels for 0%

profile of v1, /device:TPU:23, one launch (start us, length us, event | category | flops | bytes accessed | tf_op | source)
XLA Modules:
  0.0 354.9 jit_solution(4250284165621120487)
XLA Ops:
  4.5 4.7 %copy.33 = f32[9,16384]{0,1:T(8,128)} copy(f32[9,16384]{1,0:T(8,128)S(1)} %pad_maximum_fusion.1) | data formatting | bytes 1179648 | tf_op jit(solution)/shard_map/concatenate | solution.py:103
  9.4 31.2 %gather_fusion = f32[8192,9]{1,0:T(8,128)} fusion(f32[9,16384]{0,1:T(8,128)} %copy.33, s32[8192]{0:T(1024)S(1)} %broadcast_clamp_fusion.1), kind=kCustom, calls=%fused_computation | custom fusion | bytes 622592 | tf_op jit(solution)/shard_map/gather | solution.py:108
  40.6 4.2 %multiply_bitcast_fusion.1 = f32[9,8192]{0,1:T(8,128)} fusion(f32[8192,9]{1,0:T(8,128)} %gather_fusion, f32[8192]{0:T(1024)S(1)} %bitcast.189), kind=kLoop, calls=%fused_computation.160 | loop fusion | flops 73728 | bytes 622592 | tf_op jit(solution)/shard_map/mul | solution.py:108
  51.5 31.2 %gather_fusion.1 = f32[8192,9]{1,0:T(8,128)} fusion(f32[9,16384]{0,1:T(8,128)} %copy.33, s32[8192]{0:T(1024)S(1)} %broadcast_clamp_fusion), kind=kCustom, calls=%fused_computation.1 | custom fusion | bytes 622592 | tf_op jit(solution)/shard_map/gather | solution.py:109
  82.7 4.2 %multiply_bitcast_fusion = f32[9,8192]{0,1:T(8,128)} fusion(f32[8192,9]{1,0:T(8,128)} %gather_fusion.1, f32[8192]{0:T(1024)S(1)} %bitcast.188), kind=kLoop, calls=%fused_computation.159 | loop fusion | flops 73728 | bytes 622592 | tf_op jit(solution)/shard_map/mul | solution.py:109
  95.9 4.6 %fusion.120 = f32[16384]{0:T(1024)S(1)} fusion(s32[16384]{0:T(1024)S(1)} %get-tuple-element.480, pred[16384,128]{1,0:T(32,128)(4,1)S(1)} %iota_compare_fusion.22), kind=kOutput, calls=%fused_computation.179 | convolution fusion | flops 538984448 | bytes 2228224 | tf_op jit(solution)/shard_map/sh,sl->hl/dot_general | solution.py:86
  101.8 5.4 %collective-permute-done.1 = f32[9,8192]{1,0:T(8,128)} collective-permute-done((f32[9,8192]{1,0:T(8,128)}, f32[9,8192]{1,0:T(8,128)}, u32[]{:S(2)}, u32[]{:S(2)}) %collective-permute-start.1) | collective-permute-done | bytes 294944 | tf_op jit(solution)/shard_map/ppermute | solution.py:14
  109.9 86.6 %while.37 = (s32[]{:T(128)}, f32[5,128,1024]{2,1,0:T(8,128)S(1)}, f32[9,32768]{1,0:T(8,128)}, s32[256]{0:T(256)S(1)}, s32[]{:T(128)}, /*index=5*/s32[]{:T(128)},...) while((s32[]{:T(128)}, f32[5,128,1024]{2,1,0:T(8,128)S(1)}, ...), condition=%wide.region_1.2_spmd.clone, body=%wide.region_0.1_spmd.clone.sunk | while | flops 583724544 | bytes 6919223 | solution.py:134
  111.6 18.0 %fusion.174 = f32[5,64,128]{2,0,1:T(8,128)S(1)} fusion(f32[128]{0:T(128)S(1)} %compare_convert_fusion.5, f32[64,128]{1,0:T(8,128)S(1)} %bitcast.179, s32[64,128]{1,0:T(8,128)S(1)} %get-tuple-element.585, f32[64,128]{1,0:T(8,128)S(1)} %get-tuple-element.587, s32[64,128]{1,0:T(8,128)S(1)} %get-tuple-element.588, s32[128]{0:T(128)S(1)} %get-tuple-element.589, ...), kind=kOutput, calls=%fused_computation.114.clone.3 | convolution fusion | flops 78643200 | bytes 821252 | tf_op jit(solution)/shard_map/while/body/eval_jaxpr/fgp,gpe->fge/dot_general | solution.py:127
  133.2 18.0 %fusion.174 = f32[5,64,128]{2,0,1:T(8,128)S(1)} fusion(f32[128]{0:T(128)S(1)} %compare_convert_fusion.5, f32[64,128]{1,0:T(8,128)S(1)} %bitcast.179, s32[64,128]{1,0:T(8,128)S(1)} %get-tuple-element.585, f32[64,128]{1,0:T(8,128)S(1)} %get-tuple-element.587, s32[64,128]{1,0:T(8,128)S(1)} %get-tuple-element.588, s32[128]{0:T(128)S(1)} %get-tuple-element.589, ...), kind=kOutput, calls=%fused_computation.114.clone.3 | convolution fusion | flops 78643200 | bytes 821252 | tf_op jit(solution)/shard_map/while/body/eval_jaxpr/fgp,gpe->fge/dot_general | solution.py:127
  154.8 18.0 %fusion.174 = f32[5,64,128]{2,0,1:T(8,128)S(1)} fusion(f32[128]{0:T(128)S(1)} %compare_convert_fusion.5, f32[64,128]{1,0:T(8,128)S(1)} %bitcast.179, s32[64,128]{1,0:T(8,128)S(1)} %get-tuple-element.585, f32[64,128]{1,0:T(8,128)S(1)} %get-tuple-element.587, s32[64,128]{1,0:T(8,128)S(1)} %get-tuple-element.588, s32[128]{0:T(128)S(1)} %get-tuple-element.589, ...), kind=kOutput, calls=%fused_computation.114.clone.3 | convolution fusion | flops 78643200 | bytes 821252 | tf_op jit(solution)/shard_map/while/body/eval_jaxpr/fgp,gpe->fge/dot_general | solution.py:127
  176.4 18.0 %fusion.174 = f32[5,64,128]{2,0,1:T(8,128)S(1)} fusion(f32[128]{0:T(128)S(1)} %compare_convert_fusion.5, f32[64,128]{1,0:T(8,128)S(1)} %bitcast.179, s32[64,128]{1,0:T(8,128)S(1)} %get-tuple-element.585, f32[64,128]{1,0:T(8,128)S(1)} %get-tuple-element.587, s32[64,128]{1,0:T(8,128)S(1)} %get-tuple-element.588, s32[128]{0:T(128)S(1)} %get-tuple-element.589, ...), kind=kOutput, calls=%fused_computation.114.clone.3 | convolution fusion | flops 78643200 | bytes 821252 | tf_op jit(solution)/shard_map/while/body/eval_jaxpr/fgp,gpe->fge/dot_general | solution.py:127
  196.5 3.6 %reshape.681 = f32[5,25,5,16,64]{4,3,2,1,0:T(8,128)} reshape(f32[5,125,1024]{2,1,0:T(8,128)S(1)} %bitcast.165) | data formatting | bytes 5120000 | tf_op jit(solution)/shard_map/reshape | solution.py:138
  200.1 5.1 %fusion.126 = f32[5,5,5,16,256,1]{4,3,5,2,1,0:T(8,128)S(1)} fusion(f32[5,5,5,16,5,64]{5,3,4,2,1,0:T(8,128)} %bitcast.166, s32[5,64]{1,0:T(8,128)S(1)} %iota_add_fusion), kind=kOutput, calls=%fused_computation.191 | convolution fusion | flops 1966161920 | bytes 4609280 | tf_op jit(solution)/shard_map/faeyk,ekz->fayz/dot_general | solution.py:139
  208.5 8.2 %collective-permute-done.2 = f32[5,65,256]{2,1,0:T(8,128)S(1)} collective-permute-done((f32[5,65,256]{2,1,0:T(8,128)S(1)}, f32[5,65,256]{2,1,0:T(8,128)S(1)}, u32[]{:S(2)}, u32[]{:S(2)}) %collective-permute-start.2) | collective-permute-done | bytes 332832 | tf_op jit(solution)/shard_map/ppermute | solution.py:14
  228.2 10.9 %collective-permute-done.4 = f32[5,64,256]{2,1,0:T(8,128)S(1)} collective-permute-done((f32[5,64,256]{2,1,0:T(8,128)S(1)}, f32[5,64,256]{2,1,0:T(8,128)S(1)}, u32[]{:S(2)}, u32[]{:S(2)}) %collective-permute-start.4) | collective-permute-done | bytes 327712 | tf_op jit(solution)/shard_map/ppermute | solution.py:14
  244.2 4.7 %convolution_bitcast_fusion.1 = f32[5,25,5,16,64]{4,1,3,0,2:T(8,128)S(1)} fusion(f32[5,25,16,256]{3,2,1,0:T(8,128)S(1)} %bitcast.167, s32[5,64]{1,0:T(8,128)S(1)} %iota_add_fusion), kind=kOutput, calls=%fused_computation.163 | convolution fusion | flops 1966161920 | bytes 4609280 | tf_op jit(solution)/shard_map/fayz,ekz->faeyk/dot_general | solution.py:169
  248.9 5.2 %copy.44 = f32[5,25,5,16,64]{4,3,2,1,0:T(8,128)} copy(f32[5,25,5,16,64]{4,1,3,0,2:T(8,128)S(1)} %convolution_bitcast_fusion.1) | data formatting | bytes 5120000 | tf_op jit(solution)/shard_map/fayz,ekz->faeyk/transpose | solution.py:169
  254.0 5.1 %reshape.685 = f32[5,125,1024]{2,1,0:T(8,128)} reshape(f32[5,25,5,16,64]{4,3,2,1,0:T(8,128)} %copy.44) | data formatting | bytes 5120000 | tf_op jit(solution)/shard_map/reshape | solution.py:173
  261.2 92.9 %while.36 = (s32[]{:T(128)}, bf16[5,32768]{1,0:T(8,128)(2,1)S(1)}, f32[9,32768]{1,0:T(8,128)}, s32[256]{0:T(256)S(1)}, f32[5,128,1024]{2,1,0:T(8,128)S(1)}, /*in...) while((s32[]{:T(128)}, bf16[5,32768]{1,0:T(8,128)(2,1)S(1)}, ...), condition=%wide.region_3.4_spmd.clone, body=%wide.region_2.3_spmd.clone.sunk | while | flops 582454784 | bytes 4166709 | solution.py:190
  264.6 19.9 %fusion.169 = bf16[5,32768]{1,0:T(8,128)(2,1)S(1)} fusion(bf16[5,32768]{1,0:T(8,128)(2,1)S(1)} %get-tuple-element.655, s32[]{:T(128)S(6)} %select_n.843, f32[128]{0:T(128)S(1)} %compare_convert_fusion.4, f32[64,128]{1,0:T(8,128)S(1)} %bitcast.177, s32[64,128]{1,0:T(8,128)S(1)} %get-tuple-element.567, f32[64,128]{1,0:T(8,128)S(1)} %get-tuple-element.569, ...), kind=kOutput, calls=%fused_computation.39.clone.2 | convolution fusion | flops 78684160 | bytes 690180 | tf_op jit(solution)/shard_map/while/body/eval_jaxpr/fge,gpe->fgp/dot_general | solution.py:186
  287.8 19.9 %fusion.169 = bf16[5,32768]{1,0:T(8,128)(2,1)S(1)} fusion(bf16[5,32768]{1,0:T(8,128)(2,1)S(1)} %get-tuple-element.655, s32[]{:T(128)S(6)} %select_n.843, f32[128]{0:T(128)S(1)} %compare_convert_fusion.4, f32[64,128]{1,0:T(8,128)S(1)} %bitcast.177, s32[64,128]{1,0:T(8,128)S(1)} %get-tuple-element.567, f32[64,128]{1,0:T(8,128)S(1)} %get-tuple-element.569, ...), kind=kOutput, calls=%fused_computation.39.clone.2 | convolution fusion | flops 78684160 | bytes 690180 | tf_op jit(solution)/shard_map/while/body/eval_jaxpr/fge,gpe->fgp/dot_general | solution.py:186
  310.9 19.9 %fusion.169 = bf16[5,32768]{1,0:T(8,128)(2,1)S(1)} fusion(bf16[5,32768]{1,0:T(8,128)(2,1)S(1)} %get-tuple-element.655, s32[]{:T(128)S(6)} %select_n.843, f32[128]{0:T(128)S(1)} %compare_convert_fusion.4, f32[64,128]{1,0:T(8,128)S(1)} %bitcast.177, s32[64,128]{1,0:T(8,128)S(1)} %get-tuple-element.567, f32[64,128]{1,0:T(8,128)S(1)} %get-tuple-element.569, ...), kind=kOutput, calls=%fused_computation.39.clone.2 | convolution fusion | flops 78684160 | bytes 690180 | tf_op jit(solution)/shard_map/while/body/eval_jaxpr/fge,gpe->fgp/dot_general | solution.py:186
  334.2 19.9 %fusion.169 = bf16[5,32768]{1,0:T(8,128)(2,1)S(1)} fusion(bf16[5,32768]{1,0:T(8,128)(2,1)S(1)} %get-tuple-element.655, s32[]{:T(128)S(6)} %select_n.843, f32[128]{0:T(128)S(1)} %compare_convert_fusion.4, f32[64,128]{1,0:T(8,128)S(1)} %bitcast.177, s32[64,128]{1,0:T(8,128)S(1)} %get-tuple-element.567, f32[64,128]{1,0:T(8,128)S(1)} %get-tuple-element.569, ...), kind=kOutput, calls=%fused_computation.39.clone.2 | convolution fusion | flops 78684160 | bytes 690180 | tf_op jit(solution)/shard_map/while/body/eval_jaxpr/fge,gpe->fgp/dot_general | solution.py:186
  (128 shorter events, 73.5 us)
Async XLA Ops:
  48.4 53.4 %collective-permute-start = (f32[9,8192]{1,0:T(8,128)}, f32[9,8192]{1,0:T(8,128)}, u32[]{:S(2)}, u32[]{:S(2)}) collective-permute-start(f32[9,8192]{1,0:T(8,128)} %copy.34), channel_id=1, source_target_pairs={{0,2},{2,4},{4,6},{6,8},{8,10},{10,12},{12,14},{14,16},{16,18},{18... | collective-permute-start | bytes 884744 | tf_op jit(solution)/shard_map/ppermute | solution.py:14
  86.9 6.1 %copy-start.2 = (s32[2,8192]{1,0:T(2,128)S(1)}, s32[2,8192]{1,0:T(2,128)}, u32[]{:S(2)}) copy-start(s32[2,8192]{1,0:T(2,128)} %param.17) | copy-start | bytes 196612
  90.5 10.1 %copy-start.1 = (f32[3,16384]{1,0:T(4,128)S(1)}, f32[3,16384]{1,0:T(4,128)}, u32[]{:S(2)}) copy-start(f32[3,16384]{1,0:T(4,128)} %param.15) | copy-start | bytes 589828
  90.5 16.7 %collective-permute-start.1 = (f32[9,8192]{1,0:T(8,128)}, f32[9,8192]{1,0:T(8,128)}, u32[]{:S(2)}, u32[]{:S(2)}) collective-permute-start(f32[9,8192]{1,0:T(8,128)} %copy.36), channel_id=1, source_target_pairs={{2,0},{4,2},{6,4},{8,6},{10,8},{12,10},{14,12},{16,14},{18,16},{20... | collective-permute-start | bytes 884744 | tf_op jit(solution)/shard_map/ppermute | solution.py:14
  95.9 14.0 %copy-start.4 = (s32[256]{0:T(256)S(1)}, s32[256]{0:T(256)}, u32[]{:S(2)}) copy-start(s32[256]{0:T(256)} %param.18) | copy-start | bytes 3076
  206.4 10.2 %collective-permute-start.2 = (f32[5,65,256]{2,1,0:T(8,128)S(1)}, f32[5,65,256]{2,1,0:T(8,128)S(1)}, u32[]{:S(2)}, u32[]{:S(2)}) collective-permute-start(f32[5,65,256]{2,1,0:T(8,128)S(1)} %slice_bitcast_fusion), channel_id=1, source_target_pairs={{0,2},{2,4},{4,6},{6,8},{8,10},{10,12},{12,14},{14,16},{16,18},{18... | collective-permute-start | bytes 998408 | tf_op jit(solution)/shard_map/ppermute | solution.py:14
  216.7 4.7 %copy-start = (f32[5,4,65,256]{3,2,1,0:T(8,128)}, f32[5,4,65,256]{3,2,1,0:T(8,128)S(1)}, u32[]{:S(2)}) copy-start(f32[5,4,65,256]{3,2,1,0:T(8,128)S(1)} %fusion.123) | copy-start | bytes 3993604
  216.7 4.6 %collective-permute-start.3 = (f32[5,4,256]{2,1,0:T(4,128)S(1)}, f32[5,4,256]{2,1,0:T(4,128)S(1)}, u32[]{:S(2)}, u32[]{:S(2)}) collective-permute-start(f32[5,4,256]{2,1,0:T(4,128)S(1)} %bitcast.193), channel_id=1, source_target_pairs={{0,1},{2,3},{4,5},{6,7},{8,9},{10,11},{12,13},{14,15},{16,17},{18,... | collective-permute-start | bytes 61448 | tf_op jit(solution)/shard_map/ppermute | solution.py:14
  226.2 12.8 %collective-permute-start.4 = (f32[5,64,256]{2,1,0:T(8,128)S(1)}, f32[5,64,256]{2,1,0:T(8,128)S(1)}, u32[]{:S(2)}, u32[]{:S(2)}) collective-permute-start(f32[5,64,256]{2,1,0:T(8,128)S(1)} %slice_bitcast_fusion.2), channel_id=1, source_target_pairs={{2,0},{4,2},{6,4},{8,6},{10,8},{12,10},{14,12},{16,14},{18,16},{20... | collective-permute-start | bytes 983048 | tf_op jit(solution)/shard_map/ppermute | solution.py:14
  239.1 3.8 %collective-permute-start.5 = (f32[5,5,256]{2,1,0:T(8,128)S(1)}, f32[5,5,256]{2,1,0:T(8,128)S(1)}, u32[]{:S(2)}, u32[]{:S(2)}) collective-permute-start(f32[5,5,256]{2,1,0:T(8,128)S(1)} %bitcast.192), channel_id=1, source_target_pairs={{1,0},{3,2},{5,4},{7,6},{9,8},{11,10},{13,12},{15,14},{17,16},{19,... | collective-permute-start | bytes 76808 | tf_op jit(solution)/shard_map/ppermute | solution.py:14
  354.1 0.8 copy-start.3

commit v2 on v1

--- a/solution.py
+++ b/solution.py
@@ -125,10 +125,10 @@
     def deposit_turn(turn_index, brick_sums):
         block_rows, weights, selector = group_pieces(turn_index)
         spread = jnp.einsum(
-            "fgp,gpe->fge", block_rows[:5], weights, precision=lax.Precision.HIGHEST
+            "fgp,gpe->fge", block_rows[:5], weights, precision=lax.Precision.HIGH
         )
         return brick_sums + jnp.einsum(
-            "gb,fge->feb", selector, spread, precision=lax.Precision.HIGHEST
+            "gb,fge->feb", selector, spread, precision=lax.Precision.HIGH
         )
 
     brick_sums = lax.fori_loop(
@@ -137,12 +137,12 @@
     if count_x == 1:
         laid = brick_sums[:, :125].reshape(5, 25, 5, count_y, count_z)
         laid = jnp.einsum(
-            "faeyk,ekz->fayz", laid, window_map(count_z, span_z), precision=lax.Precision.HIGHEST
+            "faeyk,ekz->fayz", laid, window_map(count_z, span_z), precision=lax.Precision.HIGH
         )
         laid = laid.reshape(5, 5, 5, count_y, span_z)
         deposit_grid = jnp.einsum(
             "fxwyz,wyn->fxnz", laid, window_map(count_y, span_y + 1),
-            precision=lax.Precision.HIGHEST,
+            precision=lax.Precision.HIGH,
         )
     else:
         laid = jnp.transpose(brick_sums[:, :125], (0, 2, 1))
@@ -163,12 +163,12 @@
     if count_x == 1:
         windows = jnp.einsum(
             "fxnz,wyn->fxwyz", gas_field, window_map(count_y, span_y + 1),
-            precision=lax.Precision.HIGHEST,
+            precision=lax.Precision.HIGH,
         )
         windows = windows.reshape(5, 25, count_y, span_z)
         windows = jnp.einsum(
             "fayz,ekz->faeyk", windows, window_map(count_z, span_z),
-            precision=lax.Precision.HIGHEST,
+            precision=lax.Precision.HIGH,
         )
         windows = windows.reshape(5, 125, brick_total)
     else:
@@ -182,8 +182,8 @@
 
     def sample_turn(turn_index, sampled):
         block_rows, weights, selector = group_pieces(turn_index)
-        picked = jnp.einsum("gb,feb->fge", selector, brick_gas, precision=lax.Precision.HIGHEST)
-        values = jnp.einsum("fge,gpe->fgp", picked, weights, precision=lax.Precision.HIGHEST)
+        picked = jnp.einsum("gb,feb->fge", selector, brick_gas, precision=lax.Precision.HIGH)
+        values = jnp.einsum("fge,gpe->fgp", picked, weights, precision=lax.Precision.HIGH)
         values = values.reshape(5, group_size * 128).astype(jnp.bfloat16)
         return lax.dynamic_update_slice_in_dim(sampled, values, turn_index * group_size * 128, 1)
 

time: 356 us -> 330 us (0.927)
  matrix products: 181 us -> 155 us
    dot_general x12, matrix products: 93 us -> 76.1 us  [the longest x4 66.6 us: sample_turn(): jnp.einsum('fge,gpe->fgp', picked, weights, precision=lax.Precision.HIGH)]
    dot_general x4, matrix products: 71.8 us -> 65.2 us  [deposit_turn(): jnp.einsum('fgp,gpe->fge', block_rows[:5], weights, precision=lax.Precisi...]
  transfers between devices with their start and end apart: 6 -> 6, of which waited for: 5 -> 5; matrix products, arithmetic and copies ran while one was open for 13% -> 15% of each run, Pallas kernels for 0% -> 0%
where the time goes in v2:
time: 330 us; the launch traced here: 328 us
  matrix products  155 us (47%)
  local copies, waits for them, and re-layouts  93.8 us (28%)
  other arithmetic  35.8 us (11%)
  waiting for transfers between devices  28.6 us (9%)
  starting transfers between devices  13.6 us (4%)
    dot_general x4, matrix products, sample_turn(): jnp.einsum('fge,gpe->fgp', picked, weights, precision=lax.Precision.HIGH)  66.6 us
    dot_general x4, matrix products, deposit_turn(): jnp.einsum('fgp,gpe->fge', block_rows[:5], weights, precision=lax.Precisi...  65.2 us
    gather x1, local copies, waits for them, and re-layouts, per_device(): upward = attributes[:, safe_rows[0]] * usable[0].astype(jnp.float32)  31.2 us
    gather x1, local copies, waits for them, and re-layouts, per_device(): downward = attributes[:, safe_rows[1]] * usable[1].astype(jnp.float32)  31.2 us
    ppermute x6, waiting for transfers between devices, passed_along(): return lax.ppermute(block, axis, route)  28.6 us
    ppermute x6, starting transfers between devices, passed_along(): return lax.ppermute(block, axis, route)  13.6 us
    slice x8, other arithmetic, kernel_weights(): offsets[0]  12.4 us
  transfers between devices with their start and end apart: 6, of which 5 were waited for; matrix products, arithmetic and copies ran while one was open for 15% of the time, Pallas kernels for 0%

profile of v2, /device:TPU:23, one launch (start us, length us, event | category | flops | bytes accessed | tf_op | source)
XLA Modules:
  0.0 328.5 jit_solution(8162865065179594002)
XLA Ops:
  4.5 4.7 %copy.33 = f32[9,16384]{0,1:T(8,128)} copy(f32[9,16384]{1,0:T(8,128)S(1)} %pad_maximum_fusion.1) | data formatting | bytes 1179648 | tf_op jit(solution)/shard_map/concatenate | solution.py:103
  9.4 31.2 %gather_fusion = f32[8192,9]{1,0:T(8,128)} fusion(f32[9,16384]{0,1:T(8,128)} %copy.33, s32[8192]{0:T(1024)S(1)} %broadcast_clamp_fusion.1), kind=kCustom, calls=%fused_computation | custom fusion | bytes 622592 | tf_op jit(solution)/shard_map/gather | solution.py:108
  40.6 4.2 %multiply_bitcast_fusion.1 = f32[9,8192]{0,1:T(8,128)} fusion(f32[8192,9]{1,0:T(8,128)} %gather_fusion, f32[8192]{0:T(1024)S(1)} %bitcast.189), kind=kLoop, calls=%fused_computation.160 | loop fusion | flops 73728 | bytes 622592 | tf_op jit(solution)/shard_map/mul | solution.py:108
  51.5 31.2 %gather_fusion.1 = f32[8192,9]{1,0:T(8,128)} fusion(f32[9,16384]{0,1:T(8,128)} %copy.33, s32[8192]{0:T(1024)S(1)} %broadcast_clamp_fusion), kind=kCustom, calls=%fused_computation.1 | custom fusion | bytes 622592 | tf_op jit(solution)/shard_map/gather | solution.py:109
  82.7 4.2 %multiply_bitcast_fusion = f32[9,8192]{0,1:T(8,128)} fusion(f32[8192,9]{1,0:T(8,128)} %gather_fusion.1, f32[8192]{0:T(1024)S(1)} %bitcast.188), kind=kLoop, calls=%fused_computation.159 | loop fusion | flops 73728 | bytes 622592 | tf_op jit(solution)/shard_map/mul | solution.py:109
  86.9 3.6 %copy.36 = f32[9,8192]{1,0:T(8,128)} copy(f32[9,8192]{0,1:T(8,128)} %multiply_bitcast_fusion) | data formatting | bytes 589824 | tf_op jit(solution)/shard_map/mul | solution.py:109
  95.9 4.6 %fusion.120 = f32[16384]{0:T(1024)S(1)} fusion(s32[16384]{0:T(1024)S(1)} %get-tuple-element.480, pred[16384,128]{1,0:T(32,128)(4,1)S(1)} %iota_compare_fusion.22), kind=kOutput, calls=%fused_computation.179 | convolution fusion | flops 538984448 | bytes 2228224 | tf_op jit(solution)/shard_map/sh,sl->hl/dot_general | solution.py:86
  101.8 5.4 %collective-permute-done.1 = f32[9,8192]{1,0:T(8,128)} collective-permute-done((f32[9,8192]{1,0:T(8,128)}, f32[9,8192]{1,0:T(8,128)}, u32[]{:S(2)}, u32[]{:S(2)}) %collective-permute-start.1) | collective-permute-done | bytes 294944 | tf_op jit(solution)/shard_map/ppermute | solution.py:14
  109.9 78.6 %while.37 = (s32[]{:T(128)}, f32[5,128,1024]{2,1,0:T(8,128)S(1)}, f32[9,32768]{1,0:T(8,128)}, s32[256]{0:T(256)S(1)}, s32[]{:T(128)}, /*index=5*/s32[]{:T(128)},...) while((s32[]{:T(128)}, f32[5,128,1024]{2,1,0:T(8,128)S(1)}, ...), condition=%wide.region_1.2_spmd.clone, body=%wide.region_0.1_spmd.clone.sunk | while | flops 300609024 | bytes 6919223 | solution.py:134
  111.6 16.3 %fusion.174 = f32[5,64,128]{2,0,1:T(8,128)S(1)} fusion(f32[128]{0:T(128)S(1)} %compare_convert_fusion.5, f32[64,128]{1,0:T(8,128)S(1)} %bitcast.179, s32[64,128]{1,0:T(8,128)S(1)} %get-tuple-element.585, f32[64,128]{1,0:T(8,128)S(1)} %get-tuple-element.587, s32[64,128]{1,0:T(8,128)S(1)} %get-tuple-element.588, s32[128]{0:T(128)S(1)} %get-tuple-element.589, ...), kind=kOutput, calls=%fused_computation.114.clone.3 | convolution fusion | flops 47185920 | bytes 821252 | tf_op jit(solution)/shard_map/while/body/eval_jaxpr/fgp,gpe->fge/dot_general | solution.py:127
  131.2 16.3 %fusion.174 = f32[5,64,128]{2,0,1:T(8,128)S(1)} fusion(f32[128]{0:T(128)S(1)} %compare_convert_fusion.5, f32[64,128]{1,0:T(8,128)S(1)} %bitcast.179, s32[64,128]{1,0:T(8,128)S(1)} %get-tuple-element.585, f32[64,128]{1,0:T(8,128)S(1)} %get-tuple-element.587, s32[64,128]{1,0:T(8,128)S(1)} %get-tuple-element.588, s32[128]{0:T(128)S(1)} %get-tuple-element.589, ...), kind=kOutput, calls=%fused_computation.114.clone.3 | convolution fusion | flops 47185920 | bytes 821252 | tf_op jit(solution)/shard_map/while/body/eval_jaxpr/fgp,gpe->fge/dot_general | solution.py:127
  150.8 16.3 %fusion.174 = f32[5,64,128]{2,0,1:T(8,128)S(1)} fusion(f32[128]{0:T(128)S(1)} %compare_convert_fusion.5, f32[64,128]{1,0:T(8,128)S(1)} %bitcast.179, s32[64,128]{1,0:T(8,128)S(1)} %get-tuple-element.585, f32[64,128]{1,0:T(8,128)S(1)} %get-tuple-element.587, s32[64,128]{1,0:T(8,128)S(1)} %get-tuple-element.588, s32[128]{0:T(128)S(1)} %get-tuple-element.589, ...), kind=kOutput, calls=%fused_computation.114.clone.3 | convolution fusion | flops 47185920 | bytes 821252 | tf_op jit(solution)/shard_map/while/body/eval_jaxpr/fgp,gpe->fge/dot_general | solution.py:127
  170.4 16.3 %fusion.174 = f32[5,64,128]{2,0,1:T(8,128)S(1)} fusion(f32[128]{0:T(128)S(1)} %compare_convert_fusion.5, f32[64,128]{1,0:T(8,128)S(1)} %bitcast.179, s32[64,128]{1,0:T(8,128)S(1)} %get-tuple-element.585, f32[64,128]{1,0:T(8,128)S(1)} %get-tuple-element.587, s32[64,128]{1,0:T(8,128)S(1)} %get-tuple-element.588, s32[128]{0:T(128)S(1)} %get-tuple-element.589, ...), kind=kOutput, calls=%fused_computation.114.clone.3 | convolution fusion | flops 47185920 | bytes 821252 | tf_op jit(solution)/shard_map/while/body/eval_jaxpr/fgp,gpe->fge/dot_general | solution.py:127
  188.5 3.6 %reshape.681 = f32[5,25,5,16,64]{4,3,2,1,0:T(8,128)} reshape(f32[5,125,1024]{2,1,0:T(8,128)S(1)} %bitcast.165) | data formatting | bytes 5120000 | tf_op jit(solution)/shard_map/reshape | solution.py:138
  192.1 4.3 %fusion.126 = f32[5,5,5,16,256,1]{4,3,5,2,1,0:T(8,128)S(1)} fusion(f32[5,5,5,16,5,64]{5,3,4,2,1,0:T(8,128)} %bitcast.166, s32[5,64]{1,0:T(8,128)S(1)} %iota_add_fusion), kind=kOutput, calls=%fused_computation.191 | convolution fusion | flops 983121920 | bytes 4609280 | tf_op jit(solution)/shard_map/faeyk,ekz->fayz/dot_general | solution.py:139
  199.3 8.2 %collective-permute-done.2 = f32[5,65,256]{2,1,0:T(8,128)S(1)} collective-permute-done((f32[5,65,256]{2,1,0:T(8,128)S(1)}, f32[5,65,256]{2,1,0:T(8,128)S(1)}, u32[]{:S(2)}, u32[]{:S(2)}) %collective-permute-start.2) | collective-permute-done | bytes 332832 | tf_op jit(solution)/shard_map/ppermute | solution.py:14
  219.0 10.9 %collective-permute-done.4 = f32[5,64,256]{2,1,0:T(8,128)S(1)} collective-permute-done((f32[5,64,256]{2,1,0:T(8,128)S(1)}, f32[5,64,256]{2,1,0:T(8,128)S(1)}, u32[]{:S(2)}, u32[]{:S(2)}) %collective-permute-start.4) | collective-permute-done | bytes 327712 | tf_op jit(solution)/shard_map/ppermute | solution.py:14
  237.8 5.2 %copy.44 = f32[5,25,5,16,64]{4,3,2,1,0:T(8,128)} copy(f32[5,25,5,16,64]{4,1,3,0,2:T(8,128)S(1)} %convolution_bitcast_fusion.1) | data formatting | bytes 5120000 | tf_op jit(solution)/shard_map/fayz,ekz->faeyk/transpose | solution.py:169
  243.0 5.1 %reshape.685 = f32[5,125,1024]{2,1,0:T(8,128)} reshape(f32[5,25,5,16,64]{4,3,2,1,0:T(8,128)} %copy.44) | data formatting | bytes 5120000 | tf_op jit(solution)/shard_map/reshape | solution.py:173
  250.2 77.5 %while.36 = (s32[]{:T(128)}, bf16[5,32768]{1,0:T(8,128)(2,1)S(1)}, f32[9,32768]{1,0:T(8,128)}, s32[256]{0:T(256)S(1)}, f32[5,128,1024]{2,1,0:T(8,128)S(1)}, /*in...) while((s32[]{:T(128)}, bf16[5,32768]{1,0:T(8,128)(2,1)S(1)}, ...), condition=%wide.region_3.4_spmd.clone, body=%wide.region_2.3_spmd.clone.sunk | while | flops 299339264 | bytes 4166709 | solution.py:190
  253.0 16.6 %fusion.169 = bf16[5,32768]{1,0:T(8,128)(2,1)S(1)} fusion(bf16[5,32768]{1,0:T(8,128)(2,1)S(1)} %get-tuple-element.655, s32[]{:T(128)S(6)} %select_n.843, f32[128]{0:T(128)S(1)} %compare_convert_fusion.4, f32[64,128]{1,0:T(8,128)S(1)} %bitcast.177, s32[64,128]{1,0:T(8,128)S(1)} %get-tuple-element.567, f32[64,128]{1,0:T(8,128)S(1)} %get-tuple-element.569, ...), kind=kOutput, calls=%fused_computation.39.clone.2 | convolution fusion | flops 47226880 | bytes 690180 | tf_op jit(solution)/shard_map/while/body/eval_jaxpr/fge,gpe->fgp/dot_general | solution.py:186
  272.3 16.6 %fusion.169 = bf16[5,32768]{1,0:T(8,128)(2,1)S(1)} fusion(bf16[5,32768]{1,0:T(8,128)(2,1)S(1)} %get-tuple-element.655, s32[]{:T(128)S(6)} %select_n.843, f32[128]{0:T(128)S(1)} %compare_convert_fusion.4, f32[64,128]{1,0:T(8,128)S(1)} %bitcast.177, s32[64,128]{1,0:T(8,128)S(1)} %get-tuple-element.567, f32[64,128]{1,0:T(8,128)S(1)} %get-tuple-element.569, ...), kind=kOutput, calls=%fused_computation.39.clone.2 | convolution fusion | flops 47226880 | bytes 690180 | tf_op jit(solution)/shard_map/while/body/eval_jaxpr/fge,gpe->fgp/dot_general | solution.py:186
  291.6 16.6 %fusion.169 = bf16[5,32768]{1,0:T(8,128)(2,1)S(1)} fusion(bf16[5,32768]{1,0:T(8,128)(2,1)S(1)} %get-tuple-element.655, s32[]{:T(128)S(6)} %select_n.843, f32[128]{0:T(128)S(1)} %compare_convert_fusion.4, f32[64,128]{1,0:T(8,128)S(1)} %bitcast.177, s32[64,128]{1,0:T(8,128)S(1)} %get-tuple-element.567, f32[64,128]{1,0:T(8,128)S(1)} %get-tuple-element.569, ...), kind=kOutput, calls=%fused_computation.39.clone.2 | convolution fusion | flops 47226880 | bytes 690180 | tf_op jit(solution)/shard_map/while/body/eval_jaxpr/fge,gpe->fgp/dot_general | solution.py:186
  311.0 16.6 %fusion.169 = bf16[5,32768]{1,0:T(8,128)(2,1)S(1)} fusion(bf16[5,32768]{1,0:T(8,128)(2,1)S(1)} %get-tuple-element.655, s32[]{:T(128)S(6)} %select_n.843, f32[128]{0:T(128)S(1)} %compare_convert_fusion.4, f32[64,128]{1,0:T(8,128)S(1)} %bitcast.177, s32[64,128]{1,0:T(8,128)S(1)} %get-tuple-element.567, f32[64,128]{1,0:T(8,128)S(1)} %get-tuple-element.569, ...), kind=kOutput, calls=%fused_computation.39.clone.2 | convolution fusion | flops 47226880 | bytes 690180 | tf_op jit(solution)/shard_map/while/body/eval_jaxpr/fge,gpe->fgp/dot_general | solution.py:186
  (128 shorter events, 68.7 us)
Async XLA Ops:
  48.4 53.4 %collective-permute-start = (f32[9,8192]{1,0:T(8,128)}, f32[9,8192]{1,0:T(8,128)}, u32[]{:S(2)}, u32[]{:S(2)}) collective-permute-start(f32[9,8192]{1,0:T(8,128)} %copy.34), channel_id=1, source_target_pairs={{0,2},{2,4},{4,6},{6,8},{8,10},{10,12},{12,14},{14,16},{16,18},{18... | collective-permute-start | bytes 884744 | tf_op jit(solution)/shard_map/ppermute | solution.py:14
  86.9 6.1 %copy-start.2 = (s32[2,8192]{1,0:T(2,128)S(1)}, s32[2,8192]{1,0:T(2,128)}, u32[]{:S(2)}) copy-start(s32[2,8192]{1,0:T(2,128)} %param.17) | copy-start | bytes 196612
  90.5 10.1 %copy-start.1 = (f32[3,16384]{1,0:T(4,128)S(1)}, f32[3,16384]{1,0:T(4,128)}, u32[]{:S(2)}) copy-start(f32[3,16384]{1,0:T(4,128)} %param.15) | copy-start | bytes 589828
  90.5 16.7 %collective-permute-start.1 = (f32[9,8192]{1,0:T(8,128)}, f32[9,8192]{1,0:T(8,128)}, u32[]{:S(2)}, u32[]{:S(2)}) collective-permute-start(f32[9,8192]{1,0:T(8,128)} %copy.36), channel_id=1, source_target_pairs={{2,0},{4,2},{6,4},{8,6},{10,8},{12,10},{14,12},{16,14},{18,16},{20... | collective-permute-start | bytes 884744 | tf_op jit(solution)/shard_map/ppermute | solution.py:14
  95.9 14.0 %copy-start.4 = (s32[256]{0:T(256)S(1)}, s32[256]{0:T(256)}, u32[]{:S(2)}) copy-start(s32[256]{0:T(256)} %param.18) | copy-start | bytes 3076
  197.2 10.2 %collective-permute-start.2 = (f32[5,65,256]{2,1,0:T(8,128)S(1)}, f32[5,65,256]{2,1,0:T(8,128)S(1)}, u32[]{:S(2)}, u32[]{:S(2)}) collective-permute-start(f32[5,65,256]{2,1,0:T(8,128)S(1)} %slice_bitcast_fusion), channel_id=1, source_target_pairs={{0,2},{2,4},{4,6},{6,8},{8,10},{10,12},{12,14},{14,16},{16,18},{18... | collective-permute-start | bytes 998408 | tf_op jit(solution)/shard_map/ppermute | solution.py:14
  207.5 4.7 %copy-start = (f32[5,4,65,256]{3,2,1,0:T(8,128)}, f32[5,4,65,256]{3,2,1,0:T(8,128)S(1)}, u32[]{:S(2)}) copy-start(f32[5,4,65,256]{3,2,1,0:T(8,128)S(1)} %fusion.123) | copy-start | bytes 3993604
  207.5 4.6 %collective-permute-start.3 = (f32[5,4,256]{2,1,0:T(4,128)S(1)}, f32[5,4,256]{2,1,0:T(4,128)S(1)}, u32[]{:S(2)}, u32[]{:S(2)}) collective-permute-start(f32[5,4,256]{2,1,0:T(4,128)S(1)} %bitcast.193), channel_id=1, source_target_pairs={{0,1},{2,3},{4,5},{6,7},{8,9},{10,11},{12,13},{14,15},{16,17},{18,... | collective-permute-start | bytes 61448 | tf_op jit(solution)/shard_map/ppermute | solution.py:14
  217.0 12.8 %collective-permute-start.4 = (f32[5,64,256]{2,1,0:T(8,128)S(1)}, f32[5,64,256]{2,1,0:T(8,128)S(1)}, u32[]{:S(2)}, u32[]{:S(2)}) collective-permute-start(f32[5,64,256]{2,1,0:T(8,128)S(1)} %slice_bitcast_fusion.2), channel_id=1, source_target_pairs={{2,0},{4,2},{6,4},{8,6},{10,8},{12,10},{14,12},{16,14},{18,16},{20... | collective-permute-start | bytes 983048 | tf_op jit(solution)/shard_map/ppermute | solution.py:14
  229.9 3.8 %collective-permute-start.5 = (f32[5,5,256]{2,1,0:T(8,128)S(1)}, f32[5,5,256]{2,1,0:T(8,128)S(1)}, u32[]{:S(2)}, u32[]{:S(2)}) collective-permute-start(f32[5,5,256]{2,1,0:T(8,128)S(1)} %bitcast.192), channel_id=1, source_target_pairs={{1,0},{3,2},{5,4},{7,6},{9,8},{11,10},{13,12},{15,14},{17,16},{19,... | collective-permute-start | bytes 76808 | tf_op jit(solution)/shard_map/ppermute | solution.py:14
  327.7 0.8 copy-start.3
